TPU v7x, 256 devices: a whole 4x4x8 slice. The times are simulated.
256 devices in a mesh: elem: 32 (over z, x), blk: 8 (over y, core).
Axes of the slice: x: 4, y: 4, z: 8, core: 2. Of those that a mesh axis runs over, the one named last changes fastest.
Arguments:
- basis: bfloat16 [32768, 3, 512], P('elem'), may hold values from -6 to 6
- send_rows: int32 [32, 8, 256], P('elem', 'blk'), may hold values from 0 to 1023
- elem_slot: int32 [8, 16384], P(None, ('elem', 'blk')), may hold values from 0 to 255, as said below
- set_size: int32 [32], replicated, may hold values from 1 to 512, 10240 in all
- elem_weight: float32 [16384], P(('elem', 'blk')), may hold values from 0.2 to 5
- element_stiffening: float32 [16384], P(('elem', 'blk')), may hold values from 1 to 8
- state: bfloat16 [512], replicated, may hold values from -0.25 to 0.25
- load: float32 [512], P('blk'), may hold values from -6 to 6
Outputs:
- tangent: float32 [512, 512], P('elem', 'blk')
- residual: float32 [512], P('blk')
Inputs may be any that keep to these rules, and one draw needn't show every extreme that they name: `elem_slot`: for element column of device (s, b): p names slot p % 8 of what owner p // 8 sends to that device. From each owner only its first n slots are named, n at most 8; for every device exactly one owner gives 8, and the n over all owners sum to 128.
All inputs are finite; a program needn't handle non-finite values.
Results may differ from a plain program's by a relative error of at most 0.0003.
Values may be sent and summed in bfloat16 or wider, within the bound.
No kernel may reach another device: no remote copies, remote signals or barrier semaphores. Data moves between devices by JAX's collectives and lax.ppermute only.
A program may use at most 64 MiB of HBM per device.

v0:
```python
import jax
import jax.numpy as jnp
from jax import lax
from jax.sharding import PartitionSpec as P


def corner_grads():
    corner = jnp.arange(8)[:, None]
    bit = corner // 2 ** jnp.arange(3)[None, :] % 2
    return (bit * 2 - 1).astype(jnp.float32) * 0.25


def element_contributions(basis_matrix, displacement, stiffening_power):
    grads = corner_grads()
    element_count = basis_matrix.shape[0]
    basis_modes = basis_matrix.shape[2]
    corner_nodes = basis_matrix.reshape(element_count, 8, 3, basis_modes)
    grad_basis = jnp.einsum(
        "ak,eacm->ekcm",
        grads.astype(jnp.bfloat16),
        corner_nodes,
        preferred_element_type=jnp.float32,
    )
    moved = displacement.reshape(8, 3, element_count)
    hgrad = jnp.einsum("ak,ace->kce", grads, moved, precision=lax.Precision.HIGHEST)
    volume = hgrad[0, 0] + hgrad[1, 1] + hgrad[2, 2]
    stiff = 1.0 + stiffening_power * volume**2 - 2.0 / 3.0
    press = volume + stiffening_power * volume**3 / 3.0 - 2.0 / 3.0 * volume
    eye = jnp.eye(3, dtype=jnp.float32)
    stress = hgrad + jnp.transpose(hgrad, (1, 0, 2)) + press[None, None, :] * eye[:, :, None]
    force_vector = (
        jnp.einsum("ak,kce->ace", grads, stress, precision=lax.Precision.HIGHEST).reshape(
            24, element_count
        )
        + 0.25 * displacement
    )
    sym = grad_basis + jnp.transpose(grad_basis, (0, 2, 1, 3))
    trace_basis = grad_basis[:, 0, 0] + grad_basis[:, 1, 1] + grad_basis[:, 2, 2]
    mode_image = jnp.einsum("ak,ekcm->eacm", grads, sym, precision=lax.Precision.HIGHEST)
    mode_image = (
        mode_image
        + stiff[:, None, None, None] * grads[None, :, :, None] * trace_basis[:, None, None, :]
        + 0.25 * corner_nodes.astype(jnp.float32)
    )
    return (mode_image.reshape(element_count, 24, basis_modes), force_vector)


def local(basis, send_rows, elem_slot, set_size, elem_weight, element_stiffening, state, load):
    nodes = basis.shape[0]
    basis_modes = basis.shape[2]
    n_elem = lax.psum(1, "elem")
    n_blk = lax.psum(1, "blk")
    flat = basis.reshape(nodes, 3 * basis_modes)
    outgoing = jnp.take(flat, send_rows[0, 0], axis=0)
    arrived = lax.all_to_all(outgoing, "elem", split_axis=0, concat_axis=0, tiled=True)
    element_count = elem_slot.shape[1]
    chosen_elements = jnp.take(arrived, elem_slot.T.reshape(-1), axis=0)
    basis_matrix = chosen_elements.reshape(element_count, 24, basis_modes)
    set_index = lax.axis_index("elem")
    block_index = lax.axis_index("blk")
    live = lax.dynamic_index_in_dim(set_size, set_index, keepdims=False)
    position = block_index * element_count + jnp.arange(element_count, dtype=jnp.int32)
    weights = jnp.where(position < live, elem_weight, jnp.zeros_like(elem_weight))
    displacement = jnp.einsum("agd,d->ga", basis_matrix, state, preferred_element_type=jnp.float32)
    mode_image, force_vector = element_contributions(basis_matrix, displacement, element_stiffening)
    weighted_image = (weights[:, None, None] * mode_image).astype(jnp.bfloat16)
    weighted_force = (force_vector * weights[None, :]).astype(jnp.bfloat16)
    rows = basis_modes // n_elem
    cols = basis_modes // n_blk
    tangent = lax.dot_general(
        basis_matrix,
        weighted_image,
        (((0, 1), (0, 1)), ((), ())),
        preferred_element_type=jnp.float32,
    )
    force_all = lax.dot_general(
        basis_matrix,
        weighted_force,
        (((0, 1), (1, 0)), ((), ())),
        preferred_element_type=jnp.float32,
    )
    pad = jnp.zeros((7, basis_modes), jnp.float32)
    stacked = jnp.concatenate([tangent, force_all[None, :], pad], axis=0)
    parts = lax.all_to_all(stacked, "blk", split_axis=1, concat_axis=0, tiled=True)
    halfway = jnp.sum(parts.reshape(n_blk, basis_modes + 8, cols), axis=0)
    force_cols = halfway[basis_modes]
    tangent_rows = halfway[:basis_modes].reshape(n_elem, rows, cols)
    chunks = jnp.concatenate(
        [tangent_rows, jnp.broadcast_to(force_cols[None, None, :], (n_elem, 1, cols))], axis=1
    )
    arrived_chunks = lax.all_to_all(chunks, "elem", split_axis=0, concat_axis=0, tiled=True)
    mine = jnp.sum(arrived_chunks, axis=0)
    scale = lax.rsqrt(24.0 * jnp.sum(set_size).astype(jnp.float32))
    return (mine[:rows] * scale, mine[rows] * scale - load)


def solution(mesh):
    in_specs = (
        P("elem", None, None),
        P("elem", "blk", None),
        P(None, ("elem", "blk")),
        P(),
        P(("elem", "blk")),
        P(("elem", "blk")),
        P(),
        P("blk"),
    )
    out_specs = (P("elem", "blk"), P("blk"))
    return jax.shard_map(local, mesh=mesh, in_specs=in_specs, out_specs=out_specs, check_vma=False)
```

profile of v0, /device:TPU:1, one launch (start us, length us, event | category | flops | bytes accessed | tf_op | source)
XLA Modules:
  0.0 132.4 jit_solution(6316363443217147849)
XLA Ops:
  0.6 4.7 %copy.47 = bf16[1024,3,512]{0,2,1:T(8,128)(2,1)} copy(bf16[1024,3,512]{2,0,1:T(8,128)(2,1)} %param.8) | data formatting | bytes 6291456 | tf_op args[0]
  5.3 3.2 %copy.48 = bf16[1024,1536]{1,0:T(8,128)(2,1)S(1)} copy(bf16[1024,1536]{0,1:T(8,128)(2,1)} %bitcast.91) | data formatting | bytes 6291456 | tf_op jit(solution)/shard_map/reshape | solution.py:53
  8.6 0.5 broadcast.507
  9.1 0.7 reduce.7
  9.8 2.1 %gather_fusion = bf16[256,1536]{1,0:T(8,128)(2,1)} fusion(bf16[1024,1536]{1,0:T(8,128)(2,1)S(1)} %copy.48, s32[1024]{0:T(1024)S(1)} %pad_clamp_fusion.1), kind=kCustom, calls=%fused_computation | custom fusion | bytes 1573888 | tf_op jit(solution)/shard_map/jit(_take)/gather | solution.py:54
  12.0 2.2 %bitcast_select_fusion = bf16[32,8,1536]{2,1,0:T(8,128)(2,1)} fusion(bf16[256,1536]{1,0:T(8,128)(2,1)} %gather_fusion, pred[32,8]{1,0:T(8,128)(4,1)S(1)} %compare_and_fusion), kind=kLoop, calls=%fused_computation.21 | loop fusion | flops 393216 | bytes 1573120 | tf_op jit(solution)/shard_map/jit(_take)/select_n | solution.py:54
  14.2 11.9 %all-to-all-start = ((bf16[32,8,1536]{2,1,0:T(8,128)(2,1)}), bf16[32,8,1536]{2,1,0:T(8,128)(2,1)S(1)}, u32[]{:S(2)}, u32[]{:S(2)}) async-start(bf16[32,8,1536]{2,1,0:T(8,128)(2,1)} %bitcast_select_fusion), calls=%async_computation | async-start | bytes 1572864 | tf_op jit(solution)/shard_map/all_to_all | solution.py:55
  26.2 0.1 reshape.320
  26.3 0.1 copy.50
  26.4 0.1 copy.46
  26.5 0.3 broadcast_in_dim.61
  26.8 0.9 broadcast_in_dim.62
  27.7 0.6 dynamic_slice.4
  28.4 0.7 compare_select_fusion.10
  29.1 0.2 fusion.35
  29.3 17.8 %all-to-all-done = bf16[32,8,1536]{2,1,0:T(8,128)(2,1)S(1)} async-done(((bf16[32,8,1536]{2,1,0:T(8,128)(2,1)}), bf16[32,8,1536]{2,1,0:T(8,128)(2,1)S(1)}, u32[]{:S(2)}, u32[]{:S(2)}) %all-to-all-start) | async-done | bytes 786464 | tf_op jit(solution)/shard_map/all_to_all | solution.py:55
  47.1 2.1 %gather_fusion.1 = bf16[512,1536]{1,0:T(8,128)(2,1)S(1)} fusion(bf16[256,1536]{1,0:T(8,128)(2,1)S(1)} %bitcast.88, s32[1024]{0:T(1024)S(1)} %pad_clamp_fusion), kind=kCustom, calls=%fused_computation.1 | custom fusion | bytes 3147776 | tf_op jit(solution)/shard_map/jit(_take)/gather | solution.py:57
  49.3 1.6 %gather.18 = bf16[64,24,512]{2,1,0:T(8,128)(2,1)} reshape(bf16[512,1536]{1,0:T(8,128)(2,1)S(1)} %gather_fusion.1) | data formatting | bytes 3145728 | tf_op jit(solution)/shard_map/jit(_take)/gather | solution.py:57
  50.9 0.8 fusion.10
  51.7 1.8 %copy.93 = f32[64,3,512,3]{2,1,3,0:T(4,128)} copy(f32[64,3,512,3]{2,3,1,0:T(4,128)S(1)} %fusion.10) | data formatting | bytes 2359296 | tf_op jit(solution)/shard_map/ak,eacm->ekcm/dot_general | solution.py:18
  53.5 2.0 %bitcast_add_fusion.1 = f32[64,3,3,512]{3,2,1,0:T(4,128)} fusion(f32[64,3,512,3]{2,3,1,0:T(4,128)S(1)} %fusion.10), kind=kLoop, calls=%fused_computation.10 | loop fusion | flops 294912 | bytes 2359296 | tf_op jit(solution)/shard_map/add | solution.py:37
  55.4 1.4 %fusion.8 = bf16[512,64,24]{0,2,1:T(8,128)(2,1)} fusion(bf16[64,24,512]{2,1,0:T(8,128)(2,1)S(1)} %copy-done, pred[64,24]{1,0:T(8,128)(4,1)S(1)} %copy.46), kind=kLoop, calls=%fused_computation.15 | loop fusion | flops 786432 | bytes 3147264 | tf_op jit(solution)/shard_map/dot_general | solution.py:76
  56.8 1.5 %fusion.9 = f32[1,64,24]{2,0,1:T(1,128)S(1)} fusion(bf16[512,1,1]{0,1,2:T(2,128)(2,1)S(1)} %reshape.343, bf16[64,24,512]{2,1,0:T(8,128)(2,1)S(1)} %copy-done, pred[64,24]{1,0:T(8,128)(4,1)S(1)} %copy.46), kind=kOutput, calls=%fused_computation.16 | convolution fusion | flops 2359296 | bytes 1581568 | tf_op jit(solution)/shard_map/agd,d->ga/dot_general | solution.py:64
  58.4 0.3 fusion.20
  58.8 1.7 %slice_add_fusion = f32[64,1,1,512]{3,2,1,0:T(1,128)S(1)} fusion(f32[64,3,3,512]{3,2,1,0:T(4,128)} %bitcast.93), kind=kLoop, calls=%fused_computation.26 | loop fusion | flops 65536 | bytes 524288 | tf_op jit(solution)/shard_map/add | solution.py:38
  60.5 0.1 broadcast_multiply_fusion
  60.6 5.7 %fusion.4 = bf16[64,8,3,512]{3,1,2,0:T(8,128)(2,1)S(1)} fusion(f32[64,3,3,512]{3,2,1,0:T(4,128)} %bitcast_add_fusion.1, f32[64,512]{1,0:T(8,128)S(1)} %bitcast.95, f32[64,8,3]{1,2,0:T(4,128)S(1)} %broadcast_multiply_fusion, f32[64]{0:T(128)S(1)} %compare_select_fusion.10, bf16[64,8,3,512]{3,1,2,0:T(8,128)(2,1)S(1)} %bitcast.90, pred[64,8]{1,0:T(8,128)(4,1)S(1)} %copy.50, ...), kind=kOutput, calls=%fused_computation.7 | convolution fusion | flops 34603536 | bytes 4463416 | tf_op jit(solution)/shard_map/ak,ekcm->eacm/dot_general | solution.py:39
  66.3 1.7 %copy.54 = bf16[64,8,3,512]{3,0,2,1:T(8,128)(2,1)} copy(bf16[64,8,3,512]{3,1,2,0:T(8,128)(2,1)S(1)} %fusion.4) | data formatting | bytes 3145728 | tf_op jit(solution)/shard_map/convert_element_type | solution.py:66
  68.0 5.1 %reshape.350 = bf16[8,64,64,24]{1,0,2,3:T(8,128)(2,1)} reshape(bf16[512,64,24]{0,1,2:T(8,128)(2,1)} %bitcast.92) | data formatting | bytes 3145728 | tf_op jit(solution)/shard_map/dot_general | solution.py:70
  73.1 1.4 %broadcast_select_fusion.4 = bf16[512,1536]{1,0:T(8,128)(2,1)} fusion(pred[512,1536]{1,0:T(8,128)(4,1)S(1)} %broadcast_in_dim.62, bf16[512,1536]{1,0:T(8,128)(2,1)S(1)} %gather_fusion.1), kind=kLoop, calls=%fused_computation.24 | loop fusion | flops 786432 | bytes 3932160 | tf_op jit(solution)/shard_map/jit(_take)/select_n | solution.py:57
  74.5 2.7 %reshape.346 = bf16[64,24,512,1]{2,1,0,3:T(8,128)(2,1)S(1)} reshape(bf16[512,1536]{1,0:T(8,128)(2,1)} %broadcast_select_fusion.4) | data formatting | bytes 3145728 | tf_op jit(solution)/shard_map/jit(_take)/select_n | solution.py:57
  77.2 0.4 fusion.24
  77.7 3.0 %reshape.322 = bf16[8,64,64,24]{1,0,3,2:T(8,128)(2,1)} reshape(bf16[512,64,24]{0,2,1:T(8,128)(2,1)S(1)} %copy-done.1) | data formatting | bytes 3145728 | tf_op jit(solution)/shard_map/reshape.256
  80.8 4.5 %fusion.11 = f32[512,8,64]{0,2,1:T(8,128)S(1)} fusion(bf16[64,24,512,1]{2,1,0,3:T(8,128)(2,1)S(1)} %reshape.346, bf16[8,64,64,24]{1,0,2,3:T(8,128)(2,1)} %reshape.350), kind=kOutput, calls=%fused_computation.18 | convolution fusion | flops 805306368 | bytes 4194304 | tf_op jit(solution)/shard_map/dot_general | solution.py:70
  85.3 3.6 %fusion.14 = f32[1,8,64]{0,2,1:T(8,128)S(1)} fusion(bf16[8,64,64,24]{1,0,3,2:T(8,128)(2,1)S(1)} %copy-done.2, bf16[24,64,1,1]{1,0,2,3:T(8,128)(2,1)S(1)} %fusion.22), kind=kOutput, calls=%fused_computation.20 | convolution fusion | flops 1572864 | bytes 1577984 | tf_op jit(solution)/shard_map/dot_general | solution.py:76
  88.9 0.2 maximum_maximum_fusion
  89.1 25.0 %all_to_all.24 = f32[520,8,64]{0,2,1:T(8,128)S(1)} all-to-all(f32[520,8,64]{0,2,1:T(8,128)S(1)} %maximum_maximum_fusion), channel_id=1, replica_groups=mesh['elem'=32,'blk'=8] {'blk'}, dimensions={1} | all-to-all | bytes 2129920 | tf_op jit(solution)/shard_map/all_to_all | solution.py:84
  114.2 0.1 slice_reduce_fusion
  114.3 0.1 copy.60
  114.5 0.8 reshape.362
  115.4 4.8 %all-to-all-start.2 = ((f32[32,1,1088]{2,1,0:T(1,128)}), f32[32,1,1088]{2,1,0:T(1,128)S(1)}, u32[]{:S(2)}, u32[]{:S(2)}) async-start(f32[32,1,1088]{2,1,0:T(1,128)} %reshape.362), calls=%async_computation.2 | async-start | bytes 294912 | tf_op jit(solution)/shard_map/all_to_all | solution.py:91
  120.2 0.6 reduce_sum.29
  121.5 8.2 %all-to-all-done.2 = f32[32,1,1088]{2,1,0:T(1,128)S(1)} async-done(((f32[32,1,1088]{2,1,0:T(1,128)}), f32[32,1,1088]{2,1,0:T(1,128)S(1)}, u32[]{:S(2)}, u32[]{:S(2)}) %all-to-all-start.2) | async-done | bytes 139296 | tf_op jit(solution)/shard_map/all_to_all | solution.py:91
  129.6 0.5 broadcast.508
  130.1 1.0 reduce.8
  131.1 0.1 reshape.363
  131.3 0.6 slice_multiply_fusion
  131.9 0.5 fusion.48
  (49 shorter events, 0.7 us)
Async XLA Ops:
  5.3 3.2 %copy-start.4 = (s32[1,1,256]{2,1,0:T(1,128)S(1)}, s32[1,1,256]{2,1,0:T(1,128)}, u32[]{:S(2)}) copy-start(s32[1,1,256]{2,1,0:T(1,128)} %param.9) | copy-start | bytes 3076
  12.0 14.1 %copy-start.3 = (s32[8,64]{1,0:T(8,128)S(1)}, s32[8,64]{1,0:T(8,128)}, u32[]{:S(2)}) copy-start(s32[8,64]{1,0:T(8,128)} %param.10) | copy-start | bytes 6148
  12.0 14.6 %copy-start.5 = (bf16[512]{0:T(512)(128)(2,1)S(1)}, bf16[512]{0:T(512)(128)(2,1)}, u32[]{:S(2)}) copy-start(bf16[512]{0:T(512)(128)(2,1)} %param.14) | copy-start | bytes 3076
  14.2 32.9 %all-to-all-start = ((bf16[32,8,1536]{2,1,0:T(8,128)(2,1)}), bf16[32,8,1536]{2,1,0:T(8,128)(2,1)S(1)}, u32[]{:S(2)}, u32[]{:S(2)}) async-start(bf16[32,8,1536]{2,1,0:T(8,128)(2,1)} %bitcast_select_fusion), calls=%async_computation | async-start | bytes 1572864 | tf_op jit(solution)/shard_map/all_to_all | solution.py:55
  26.1 1.6 %copy-start.9 = (s32[32]{0:T(128)S(1)}, s32[32]{0:T(128)}, u32[]{:S(2)}) copy-start(s32[32]{0:T(128)} %param.11) | copy-start | bytes 388
  26.1 2.4 %copy-start.6 = (f32[64]{0:T(128)S(1)}, f32[64]{0:T(128)}, u32[]{:S(2)}) copy-start(f32[64]{0:T(128)} %param.12) | copy-start | bytes 772
  53.5 2.0 %copy-start = (bf16[64,24,512]{2,1,0:T(8,128)(2,1)S(1)}, bf16[64,24,512]{2,1,0:T(8,128)(2,1)}, u32[]{:S(2)}) copy-start(bf16[64,24,512]{2,1,0:T(8,128)(2,1)} %gather.18) | copy-start | bytes 4718596
  56.8 3.6 %copy-start.7 = (f32[64]{0:T(128)S(1)}, f32[64]{0:T(128)}, u32[]{:S(2)}) copy-start(f32[64]{0:T(128)} %param.13) | copy-start | bytes 772
  74.5 3.2 %copy-start.1 = (bf16[512,64,24]{0,2,1:T(8,128)(2,1)S(1)}, bf16[512,64,24]{0,2,1:T(8,128)(2,1)}, u32[]{:S(2)}) copy-start(bf16[512,64,24]{0,2,1:T(8,128)(2,1)} %fusion.8) | copy-start | bytes 4718596
  80.8 4.5 %copy-start.2 = (bf16[8,64,64,24]{1,0,3,2:T(8,128)(2,1)S(1)}, bf16[8,64,64,24]{1,0,3,2:T(8,128)(2,1)}, u32[]{:S(2)}) copy-start(bf16[8,64,64,24]{1,0,3,2:T(8,128)(2,1)} %reshape.322) | copy-start | bytes 4718596
  114.3 17.6 %copy-start.8 = (f32[64]{0:T(128)S(1)}, f32[64]{0:T(128)}, u32[]{:S(2)}) copy-start(f32[64]{0:T(128)} %param.15) | copy-start | bytes 772
  115.4 14.3 %all-to-all-start.2 = ((f32[32,1,1088]{2,1,0:T(1,128)}), f32[32,1,1088]{2,1,0:T(1,128)S(1)}, u32[]{:S(2)}, u32[]{:S(2)}) async-start(f32[32,1,1088]{2,1,0:T(1,128)} %reshape.362), calls=%async_computation.2 | async-start | bytes 294912 | tf_op jit(solution)/shard_map/all_to_all | solution.py:91
where the time goes:
time: 133 us; the launch traced here: 132 us
  local copies, waits for them, and re-layouts  32.8 us (25%)
  waiting for transfers between devices  26 us (20%)
  blocking collectives  25 us (19%)
  matrix products  16.9 us (13%)
  starting transfers between devices  16.7 us (13%)
  other arithmetic  13.4 us (10%)
  between operations  1.7 us (1%)
    all_to_all x1, blocking collectives, local(): lax.all_to_all(stacked, 'blk', split_axis=1, concat_axis=0, tiled=True)  25 us
    all_to_all x1, waiting for transfers between devices, local(): lax.all_to_all(outgoing, 'elem', split_axis=0, concat_axis=0, tiled=True)  17.8 us
    all_to_all x1, starting transfers between devices, local(): lax.all_to_all(outgoing, 'elem', split_axis=0, concat_axis=0, tiled=True)  11.9 us
    all_to_all x1, waiting for transfers between devices, local(): lax.all_to_all(chunks, 'elem', split_axis=0, concat_axis=0, tiled=True)  8.16 us
    unnamed x26, local copies, waits for them, and re-layouts  6.21 us
    dot_general x1, matrix products, element_contributions(): jnp.einsum('ak,ekcm->eacm', grads, sym, precision=lax.Precision.HIGHEST)  5.69 us
    dot_general x1, local copies, waits for them, and re-layouts, local(): lax.dot_general(basis_matrix, weighted_image, (((0, 1), (0, 1)), ((), ())...  5.14 us
    all_to_all x1, starting transfers between devices, local(): lax.all_to_all(chunks, 'elem', split_axis=0, concat_axis=0, tiled=True)  4.79 us
  transfers between devices with their start and end apart: 2, of which 2 were waited for; matrix products, arithmetic and copies ran while one was open for 3% of the time, Pallas kernels for 0%

commit v1 on v0

--- a/solution.py
+++ b/solution.py
@@ -81,7 +81,10 @@
     )
     pad = jnp.zeros((7, basis_modes), jnp.float32)
     stacked = jnp.concatenate([tangent, force_all[None, :], pad], axis=0)
-    parts = lax.all_to_all(stacked, "blk", split_axis=1, concat_axis=0, tiled=True)
+    size = lax.axis_size("blk")
+    blocks = jnp.stack(jnp.split(stacked, size, axis=1), axis=0)
+    blocks = lax.all_to_all(blocks, "blk", split_axis=0, concat_axis=0)
+    parts = jnp.concatenate(blocks, axis=0)
     halfway = jnp.sum(parts.reshape(n_blk, basis_modes + 8, cols), axis=0)
     force_cols = halfway[basis_modes]
     tangent_rows = halfway[:basis_modes].reshape(n_elem, rows, cols)

time: 133 us -> 122 us (0.917)
  matrix products: 16.9 us -> 11.7 us
  local copies, waits for them, and re-layouts: 32.8 us -> 28.3 us
  other arithmetic: 13.4 us -> 11.9 us
    dot_general x1 -> x0, local copies, waits for them, and re-layouts: 5.14 us -> none  [local(): lax.dot_general(basis_matrix, weighted_image, (((0, 1), (0, 1)), ((), ())...]
    dot_general x1, matrix products: 3.62 us -> 0.44 us  [local(): lax.dot_general(basis_matrix, weighted_force, (((0, 1), (1, 0)), ((), ())...]
    another operation x1 -> x2, local copies, waits for them, and re-layouts: 3.04 us -> 1.09 us  [local(): blocks = jnp.stack(jnp.split(stacked, size, axis=1), axis=0)]
    dot_general x1, matrix products: 4.54 us -> 2.65 us  [local(): lax.dot_general(basis_matrix, weighted_image, (((0, 1), (0, 1)), ((), ())...]
    dot_general x1 -> x0, other arithmetic: 1.41 us -> none  [local(): lax.dot_general(basis_matrix, weighted_force, (((0, 1), (1, 0)), ((), ())...]
    unnamed x26 -> x33, local copies, waits for them, and re-layouts: 6.21 us -> 7.55 us
where the time goes in v1:
time: 122 us; the launch traced here: 121 us
  local copies, waits for them, and re-layouts  28.3 us (23%)
  waiting for transfers between devices  26 us (21%)
  blocking collectives  25 us (20%)
  starting transfers between devices  16.7 us (14%)
  other arithmetic  11.9 us (10%)
  matrix products  11.7 us (10%)
  between operations  1.76 us (1%)
    all_to_all x1, blocking collectives, local(): blocks = lax.all_to_all(blocks, 'blk', split_axis=0, concat_axis=0)  25 us
    all_to_all x1, waiting for transfers between devices, local(): lax.all_to_all(outgoing, 'elem', split_axis=0, concat_axis=0, tiled=True)  17.8 us
    all_to_all x1, starting transfers between devices, local(): lax.all_to_all(outgoing, 'elem', split_axis=0, concat_axis=0, tiled=True)  11.9 us
    all_to_all x1, waiting for transfers between devices, local(): lax.all_to_all(chunks, 'elem', split_axis=0, concat_axis=0, tiled=True)  8.16 us
    unnamed x33, local copies, waits for them, and re-layouts  7.55 us
    dot_general x1, matrix products, element_contributions(): jnp.einsum('ak,ekcm->eacm', grads, sym, precision=lax.Precision.HIGHEST)  5.61 us
    all_to_all x1, starting transfers between devices, local(): lax.all_to_all(chunks, 'elem', split_axis=0, concat_axis=0, tiled=True)  4.8 us
    select_n x1, local copies, waits for them, and re-layouts, local(): chosen_elements = jnp.take(arrived, elem_slot.T.reshape(-1), axis=0)  3.81 us
  transfers between devices with their start and end apart: 2, of which 2 were waited for; matrix products, arithmetic and copies ran while one was open for 3% of the time, Pallas kernels for 0%

profile of v1, /device:TPU:1, one launch (start us, length us, event | category | flops | bytes accessed | tf_op | source)
XLA Modules:
  0.0 121.3 jit_solution(9407260219563906919)
XLA Ops:
  0.6 4.7 %copy.56 = bf16[1024,3,512]{0,2,1:T(8,128)(2,1)} copy(bf16[1024,3,512]{2,0,1:T(8,128)(2,1)} %param.8) | data formatting | bytes 6291456 | tf_op args[0]
  5.3 3.2 %copy.57 = bf16[1024,1536]{1,0:T(8,128)(2,1)S(1)} copy(bf16[1024,1536]{0,1:T(8,128)(2,1)} %bitcast.111) | data formatting | bytes 6291456 | tf_op jit(solution)/shard_map/reshape | solution.py:53
  8.6 0.5 broadcast.506
  9.1 0.7 reduce.5
  9.8 2.1 %gather_fusion = bf16[256,1536]{1,0:T(8,128)(2,1)} fusion(bf16[1024,1536]{1,0:T(8,128)(2,1)S(1)} %copy.57, s32[1024]{0:T(1024)S(1)} %pad_clamp_fusion.1), kind=kCustom, calls=%fused_computation | custom fusion | bytes 1573888 | tf_op jit(solution)/shard_map/jit(_take)/gather | solution.py:54
  12.0 2.2 %bitcast_select_fusion = bf16[32,8,1536]{2,1,0:T(8,128)(2,1)} fusion(bf16[256,1536]{1,0:T(8,128)(2,1)} %gather_fusion, pred[32,8]{1,0:T(8,128)(4,1)S(1)} %compare_and_fusion), kind=kLoop, calls=%fused_computation.19 | loop fusion | flops 393216 | bytes 1573120 | tf_op jit(solution)/shard_map/jit(_take)/select_n | solution.py:54
  14.2 11.9 %all-to-all-start = ((bf16[32,8,1536]{2,1,0:T(8,128)(2,1)}), bf16[32,8,1536]{2,1,0:T(8,128)(2,1)S(1)}, u32[]{:S(2)}, u32[]{:S(2)}) async-start(bf16[32,8,1536]{2,1,0:T(8,128)(2,1)} %bitcast_select_fusion), calls=%async_computation | async-start | bytes 1572864 | tf_op jit(solution)/shard_map/all_to_all | solution.py:55
  26.3 0.1 copy.59
  26.4 0.1 copy.55
  26.5 0.3 broadcast_in_dim.63
  26.8 0.9 broadcast_in_dim.64
  27.7 0.6 dynamic_slice.4
  28.4 0.7 compare_select_fusion.10
  29.1 0.2 fusion.39
  29.3 17.8 %all-to-all-done = bf16[32,8,1536]{2,1,0:T(8,128)(2,1)S(1)} async-done(((bf16[32,8,1536]{2,1,0:T(8,128)(2,1)}), bf16[32,8,1536]{2,1,0:T(8,128)(2,1)S(1)}, u32[]{:S(2)}, u32[]{:S(2)}) %all-to-all-start) | async-done | bytes 786464 | tf_op jit(solution)/shard_map/all_to_all | solution.py:55
  47.1 2.1 %gather_fusion.1 = bf16[512,1536]{1,0:T(8,128)(2,1)S(1)} fusion(bf16[256,1536]{1,0:T(8,128)(2,1)S(1)} %bitcast.108, s32[1024]{0:T(1024)S(1)} %pad_clamp_fusion), kind=kCustom, calls=%fused_computation.1 | custom fusion | bytes 3147776 | tf_op jit(solution)/shard_map/jit(_take)/gather | solution.py:57
  49.3 1.7 %gather.18 = bf16[64,24,512]{2,1,0:T(8,128)(2,1)} reshape(bf16[512,1536]{1,0:T(8,128)(2,1)S(1)} %gather_fusion.1) | data formatting | bytes 3145728 | tf_op jit(solution)/shard_map/jit(_take)/gather | solution.py:57
  50.9 0.8 fusion.8
  51.7 1.8 %copy.90 = f32[64,3,512,3]{2,1,3,0:T(4,128)} copy(f32[64,3,512,3]{2,3,1,0:T(4,128)S(1)} %fusion.8) | data formatting | bytes 2359296 | tf_op jit(solution)/shard_map/ak,eacm->ekcm/dot_general | solution.py:18
  53.5 1.9 %bitcast_add_fusion.1 = f32[64,3,3,512]{3,2,1,0:T(4,128)} fusion(f32[64,3,512,3]{2,3,1,0:T(4,128)S(1)} %fusion.8), kind=kLoop, calls=%fused_computation.6 | loop fusion | flops 294912 | bytes 2359296 | tf_op jit(solution)/shard_map/add | solution.py:37
  55.4 1.5 %fusion.7 = f32[1,64,24]{2,0,1:T(1,128)S(1)} fusion(bf16[512,1,1]{0,1,2:T(2,128)(2,1)S(1)} %reshape.326, bf16[64,24,512]{2,1,0:T(8,128)(2,1)S(1)} %copy-done, pred[64,24]{1,0:T(8,128)(4,1)S(1)} %copy.55), kind=kOutput, calls=%fused_computation.14 | convolution fusion | flops 2359296 | bytes 1581568 | tf_op jit(solution)/shard_map/agd,d->ga/dot_general | solution.py:64
  57.0 0.3 fusion.24
  57.4 1.7 %slice_add_fusion = f32[64,1,1,512]{3,2,1,0:T(1,128)S(1)} fusion(f32[64,3,3,512]{3,2,1,0:T(4,128)} %bitcast.112), kind=kLoop, calls=%fused_computation.41 | loop fusion | flops 65536 | bytes 524288 | tf_op jit(solution)/shard_map/add | solution.py:38
  59.1 0.1 broadcast_multiply_fusion
  59.2 5.6 %fusion.2 = bf16[64,8,3,512]{3,1,2,0:T(8,128)(2,1)S(1)} fusion(f32[64,3,3,512]{3,2,1,0:T(4,128)} %bitcast_add_fusion.1, f32[64,512]{1,0:T(8,128)S(1)} %bitcast.115, f32[64,8,3]{1,2,0:T(4,128)S(1)} %broadcast_multiply_fusion, f32[64]{0:T(128)S(1)} %compare_select_fusion.10, bf16[64,8,3,512]{3,1,2,0:T(8,128)(2,1)S(1)} %bitcast.110, ...), kind=kOutput, calls=%fused_computation.5 | convolution fusion | flops 34603536 | bytes 4463416 | tf_op jit(solution)/shard_map/ak,ekcm->eacm/dot_general | solution.py:39
  64.8 1.7 %copy.63 = bf16[64,8,3,512]{3,0,2,1:T(8,128)(2,1)} copy(bf16[64,8,3,512]{3,1,2,0:T(8,128)(2,1)S(1)} %fusion.2) | data formatting | bytes 3145728 | tf_op jit(solution)/shard_map/convert_element_type | solution.py:66
  66.5 1.4 %broadcast_select_fusion.7 = bf16[512,1536]{1,0:T(8,128)(2,1)} fusion(pred[512,1536]{1,0:T(8,128)(4,1)S(1)} %broadcast_in_dim.64, bf16[512,1536]{1,0:T(8,128)(2,1)S(1)} %gather_fusion.1), kind=kLoop, calls=%fused_computation.23 | loop fusion | flops 786432 | bytes 3932160 | tf_op jit(solution)/shard_map/jit(_take)/select_n | solution.py:57
  67.9 3.8 %select_n.226 = bf16[64,24,512]{2,1,0:T(8,128)(2,1)} reshape(bf16[512,1536]{1,0:T(8,128)(2,1)} %broadcast_select_fusion.7) | data formatting | bytes 3145728 | tf_op jit(solution)/shard_map/jit(_take)/select_n | solution.py:57
  71.7 0.4 fusion.28
  72.3 0.4 fusion.12
  72.7 0.8 copy-done.2
  73.5 2.7 %fusion.9 = f32[512,512]{1,0:T(8,128)S(1)} fusion(bf16[64,24,512]{2,1,0:T(8,128)(2,1)} %select_n.226, bf16[64,24,512]{2,0,1:T(8,128)(2,1)S(1)} %bitcast.113), kind=kOutput, calls=%fused_computation.16 | convolution fusion | flops 805306368 | bytes 4194304 | tf_op jit(solution)/shard_map/dot_general | solution.py:70
  76.2 0.1 maximum_maximum_fusion
  76.4 0.1 fusion.22
  76.6 0.1 fusion.20
  76.7 0.1 fusion.18
  76.9 0.1 fusion.16
  77.1 1.0 copy.67
  78.0 25.0 %all_to_all.19 = f32[8,520,64]{1,2,0:T(8,128)S(1)} all-to-all(f32[8,520,64]{1,2,0:T(8,128)S(1)} %copy.67), channel_id=1, replica_groups=mesh['elem'=32,'blk'=8] {'blk'}, dimensions={0} | all-to-all | bytes 2129920 | tf_op jit(solution)/shard_map/all_to_all | solution.py:86
  103.2 0.1 copy.68
  103.4 0.8 reshape.342
  104.3 4.8 %all-to-all-start.2 = ((f32[32,1,1088]{2,1,0:T(1,128)}), f32[32,1,1088]{2,1,0:T(1,128)S(1)}, u32[]{:S(2)}, u32[]{:S(2)}) async-start(f32[32,1,1088]{2,1,0:T(1,128)} %reshape.342), calls=%async_computation.2 | async-start | bytes 294912 | tf_op jit(solution)/shard_map/all_to_all | solution.py:94
  109.1 0.6 reduce_sum.29
  110.4 8.2 %all-to-all-done.2 = f32[32,1,1088]{2,1,0:T(1,128)S(1)} async-done(((f32[32,1,1088]{2,1,0:T(1,128)}), f32[32,1,1088]{2,1,0:T(1,128)S(1)}, u32[]{:S(2)}, u32[]{:S(2)}) %all-to-all-start.2) | async-done | bytes 139296 | tf_op jit(solution)/shard_map/all_to_all | solution.py:94
  118.6 0.5 broadcast.507
  119.1 1.0 reduce.6
  120.2 0.6 slice_multiply_fusion
  120.8 0.5 fusion.52
  (56 shorter events, 1.3 us)
Async XLA Ops:
  5.3 3.2 %copy-start.4 = (s32[1,1,256]{2,1,0:T(1,128)S(1)}, s32[1,1,256]{2,1,0:T(1,128)}, u32[]{:S(2)}) copy-start(s32[1,1,256]{2,1,0:T(1,128)} %param.9) | copy-start | bytes 3076
  12.0 14.1 %copy-start.3 = (s32[8,64]{1,0:T(8,128)S(1)}, s32[8,64]{1,0:T(8,128)}, u32[]{:S(2)}) copy-start(s32[8,64]{1,0:T(8,128)} %param.10) | copy-start | bytes 6148
  12.0 14.6 %copy-start.5 = (bf16[512]{0:T(512)(128)(2,1)S(1)}, bf16[512]{0:T(512)(128)(2,1)}, u32[]{:S(2)}) copy-start(bf16[512]{0:T(512)(128)(2,1)} %param.14) | copy-start | bytes 3076
  14.2 32.9 %all-to-all-start = ((bf16[32,8,1536]{2,1,0:T(8,128)(2,1)}), bf16[32,8,1536]{2,1,0:T(8,128)(2,1)S(1)}, u32[]{:S(2)}, u32[]{:S(2)}) async-start(bf16[32,8,1536]{2,1,0:T(8,128)(2,1)} %bitcast_select_fusion), calls=%async_computation | async-start | bytes 1572864 | tf_op jit(solution)/shard_map/all_to_all | solution.py:55
  26.1 1.6 %copy-start.9 = (s32[32]{0:T(128)S(1)}, s32[32]{0:T(128)}, u32[]{:S(2)}) copy-start(s32[32]{0:T(128)} %param.11) | copy-start | bytes 388
  26.1 2.4 %copy-start.6 = (f32[64]{0:T(128)S(1)}, f32[64]{0:T(128)}, u32[]{:S(2)}) copy-start(f32[64]{0:T(128)} %param.12) | copy-start | bytes 772
  53.5 1.9 %copy-start = (bf16[64,24,512]{2,1,0:T(8,128)(2,1)S(1)}, bf16[64,24,512]{2,1,0:T(8,128)(2,1)}, u32[]{:S(2)}) copy-start(bf16[64,24,512]{2,1,0:T(8,128)(2,1)} %gather.18) | copy-start | bytes 4718596
  55.4 3.6 %copy-start.7 = (f32[64]{0:T(128)S(1)}, f32[64]{0:T(128)}, u32[]{:S(2)}) copy-start(f32[64]{0:T(128)} %param.13) | copy-start | bytes 772
  67.8 4.4 %copy-start.1 = (bf16[64,24,512]{2,1,0:T(8,128)(2,1)S(1)}, bf16[64,24,512]{2,1,0:T(8,128)(2,1)}, u32[]{:S(2)}) copy-start(bf16[64,24,512]{2,1,0:T(8,128)(2,1)} %gather.18) | copy-start | bytes 4718596
  72.1 1.4 %copy-start.2 = (bf16[64,8,3,512]{3,0,2,1:T(8,128)(2,1)S(1)}, bf16[64,8,3,512]{3,0,2,1:T(8,128)(2,1)}, u32[]{:S(2)}) copy-start(bf16[64,8,3,512]{3,0,2,1:T(8,128)(2,1)} %copy.63) | copy-start | bytes 4718596
  103.2 17.6 %copy-start.8 = (f32[64]{0:T(128)S(1)}, f32[64]{0:T(128)}, u32[]{:S(2)}) copy-start(f32[64]{0:T(128)} %param.15) | copy-start | bytes 772
  104.3 14.3 %all-to-all-start.2 = ((f32[32,1,1088]{2,1,0:T(1,128)}), f32[32,1,1088]{2,1,0:T(1,128)S(1)}, u32[]{:S(2)}, u32[]{:S(2)}) async-start(f32[32,1,1088]{2,1,0:T(1,128)} %reshape.342), calls=%async_computation.2 | async-start | bytes 294912 | tf_op jit(solution)/shard_map/all_to_all | solution.py:94
